TPU v7x, 512 devices: a whole 4x4x16 slice. The times are simulated.
512 devices in a mesh: cuts: 16 (over z_lo, core), stem: 32 (over z_hi, x, y).
Axes of the slice: x: 4, y: 4, z: 16 (z_hi: 2, z_lo: 8; z = z_hi * 8 + z_lo), core: 2. Of those that a mesh axis runs over, the one named last changes fastest.
Arguments:
- stem_tensor: bfloat16 [32, 16384, 2, 512], P('cuts', 'stem'), may hold values from -6 to 6
- branch_tensor: bfloat16 [32, 512, 2, 512], P('cuts', 'stem'), may hold values from -0.1875 to 0.1875
- open_tensor: bfloat16 [32, 16384, 2, 512], P('cuts', 'stem'), may hold values from -0.75 to 0.75
- open_order: int32 [32, 512], P('cuts'), may hold values from 0 to 511, each once within a row
Outputs:
- amplitudes: float32 [32, 512, 2, 512], P('stem', 'cuts')
Inputs may be any that keep to these rules, and one draw needn't show every extreme that they name: Each row of open_order holds every number of 0 to 511 once.
All inputs are finite; a program needn't handle non-finite values.
Results may differ from a plain program's by a relative error of at most 0.0003.
Values may be sent and summed in bfloat16 or wider, within the bound.
No kernel may reach another device: no remote copies, remote signals or barrier semaphores. Data moves between devices by JAX's collectives and lax.ppermute only.
A program may use at most 64 MiB of HBM per device.

v0:
```python
from functools import partial
import jax
import jax.numpy as jnp
from jax import lax
from jax.sharding import PartitionSpec as P


def from_behind(value, axis, steps):
    count = lax.axis_size(axis)
    pairs = [(source, (source + steps) % count) for source in range(count)]
    return lax.ppermute(value, axis, pairs)


def expand_branch(segment):
    top_rows = jnp.concatenate([segment[..., 0, :], segment[..., 1, :]], axis=-1)
    bottom_rows = jnp.concatenate([-segment[..., 1, :], segment[..., 0, :]], axis=-1)
    return jnp.concatenate([top_rows, bottom_rows], axis=-2)


def fold_rows(stem_block, running, segment, offset):
    stem_cols = stem_block
    stem_cols = stem_cols.reshape(stem_cols.shape[0], -1)
    product = jnp.dot(stem_cols, expand_branch(segment), preferred_element_type=jnp.float32)
    return product.reshape(running.shape)


def body(stem_tensor, branch_tensor, open_tensor, open_order):
    slice_count = stem_tensor.shape[0]
    row_count = stem_tensor.shape[1]
    width = stem_tensor.shape[3]
    image_list = []
    for slice_pos in range(slice_count):
        initial = jnp.zeros((row_count, 2, width), jnp.float32)
        folder = partial(fold_rows, stem_tensor[slice_pos])
        image_list.append(
            folder(
                initial,
                lax.all_gather(branch_tensor[slice_pos], "stem", axis=0, tiled=True),
                jnp.int32(0),
            )
        )
    local_sum = jnp.zeros((row_count, 2, width), jnp.float32)
    for slice_pos in range(slice_count):
        placed = jnp.take(image_list[slice_pos], open_order[slice_pos], axis=2)
        opened = open_tensor[slice_pos].astype(jnp.float32)
        real_part = placed[:, 0, :] * opened[:, 0, :] - placed[:, 1, :] * opened[:, 1, :]
        imag_part = placed[:, 0, :] * opened[:, 1, :] + placed[:, 1, :] * opened[:, 0, :]
        local_sum = local_sum + jnp.stack([real_part, imag_part], axis=1)
    cut_count = lax.axis_size("cuts")
    block_rows = row_count // cut_count
    cut_index = lax.axis_index("cuts")

    def pick_block(turn):
        start_row = (cut_index + cut_count - 1 - turn) % cut_count * block_rows
        return lax.dynamic_slice_in_dim(local_sum, start_row, block_rows, 0)

    def pass_along(turn, running):
        return from_behind(running, "cuts", 1) + pick_block(turn)

    running = lax.fori_loop(1, cut_count, pass_along, pick_block(0))
    return running.reshape(1, block_rows, 2, width)


def solution(mesh):
    return jax.shard_map(
        body,
        mesh=mesh,
        in_specs=(
            P("cuts", "stem", None, None),
            P("cuts", "stem", None, None),
            P("cuts", "stem", None, None),
            P("cuts", None),
        ),
        out_specs=P("stem", "cuts", None, None),
        check_vma=False,
    )
```

profile of v0, /device:TPU:2, one launch (start us, length us, event | category | flops | bytes accessed | tf_op | source)
XLA Modules:
  0.0 490.7 jit_solution(4633315407787686485)
XLA Ops:
  8.8 2.8 fusion.20
  11.7 2.3 fusion.21
  16.5 2.1 copy.18
  18.6 2.1 copy.16
  20.8 2.1 bitcast_convert_fusion
  22.9 2.0 bitcast_convert_fusion.1
  24.9 103.1 %all-gather.7.cloned.1.call-done = bf16[1,512,2,512]{3,1,2,0:T(8,128)(2,1)} async-done(((bf16[1,16,2,512]{3,1,2,0:T(8,128)(2,1)}), bf16[1,512,2,512]{3,1,2,0:T(8,128)(2,1)}) %all-gather.7.cloned.1.call-update) | async-done | bytes 1048592 | tf_op jit(solution)/shard_map/all_gather | solution.py:38
  130.4 104.0 %all-gather.5.cloned.1.call-done = bf16[1,512,2,512]{3,1,2,0:T(8,128)(2,1)} async-done(((bf16[1,16,2,512]{3,1,2,0:T(8,128)(2,1)}), bf16[1,512,2,512]{3,1,2,0:T(8,128)(2,1)}) %all-gather.5.cloned.1.call-update) | async-done | bytes 1048592 | tf_op jit(solution)/shard_map/all_gather | solution.py:38
  240.2 3.0 copy.8
  243.2 4.4 gather_fusion.1
  247.6 4.2 select_bitcast_fusion
  251.7 4.3 gather_fusion
  256.1 3.2 select_bitcast_fusion.1
  259.2 7.4 %multiply_subtract_fusion = (f32[512,1,512]{0,1,2:T(1,128)S(1)}, f32[512,1,512]{0,1,2:T(1,128)S(1)}, f32[512,1,512]{0,1,2:T(1,128)S(1)}, f32[512,1,512]{0,1,2:T(1,128)S(1)}) fusion(f32[512,2,512]{0,1,2:T(2,128)S(1)} %copy-done.1, f32[512,2,512]{0,1,2:T(2,128)} %select_bitcast_fusion, f32[512,2,512]{0,1,2:T(2,128)S(1)} %copy-done.2, ...), kind=kLoop, calls=%fused_computation.25 | loop fusion | flops 3145728 | bytes 12582912 | tf_op jit(solution)/shard_map/sub | solution.py:46
  266.7 3.5 maximum_add_fusion
  270.1 4.1 copy.14
  275.0 208.2 %while.15 = (s32[]{:T(128)}, f32[32,2,512]{2,1,0:T(2,128)S(1)}, s32[]{:T(128)}, f32[512,2,512]{2,1,0:T(2,128)}, s32[]{:T(128)}, /*index=5*/s32[]{:T(128)}, s32[]{:T(128)}, s32[]{:T(128)}, s32[]{:T(128)}, s32[]{:T(128)}) while((s32[]{:T(128)}, f32[32,2,512]{2,1,0:T(2,128)S(1)}, s32[]{:T(128)}, f32[512,2,512]{2,1,0:T(2,128)}, s32[]{:T(128)}, ...), condition=%wide.region_1.3_spmd, body=%wide.region_0.0_spmd.sunk | while | flops 32786 | bytes 917816 | solution.py:60
  277.0 10.9 %collective-permute-done = f32[32,2,512]{2,1,0:T(2,128)S(1)} collective-permute-done((f32[32,2,512]{2,1,0:T(2,128)S(1)}, f32[32,2,512]{2,1,0:T(2,128)S(1)}, u32[]{:S(2)}, u32[]{:S(2)}) %collective-permute-start) | collective-permute-done | bytes 131104 | tf_op jit(solution)/shard_map/while/body/eval_jaxpr/ppermute | solution.py:11
  290.9 10.9 %collective-permute-done = f32[32,2,512]{2,1,0:T(2,128)S(1)} collective-permute-done((f32[32,2,512]{2,1,0:T(2,128)S(1)}, f32[32,2,512]{2,1,0:T(2,128)S(1)}, u32[]{:S(2)}, u32[]{:S(2)}) %collective-permute-start) | collective-permute-done | bytes 131104 | tf_op jit(solution)/shard_map/while/body/eval_jaxpr/ppermute | solution.py:11
  304.8 10.9 %collective-permute-done = f32[32,2,512]{2,1,0:T(2,128)S(1)} collective-permute-done((f32[32,2,512]{2,1,0:T(2,128)S(1)}, f32[32,2,512]{2,1,0:T(2,128)S(1)}, u32[]{:S(2)}, u32[]{:S(2)}) %collective-permute-start) | collective-permute-done | bytes 131104 | tf_op jit(solution)/shard_map/while/body/eval_jaxpr/ppermute | solution.py:11
  318.6 10.9 %collective-permute-done = f32[32,2,512]{2,1,0:T(2,128)S(1)} collective-permute-done((f32[32,2,512]{2,1,0:T(2,128)S(1)}, f32[32,2,512]{2,1,0:T(2,128)S(1)}, u32[]{:S(2)}, u32[]{:S(2)}) %collective-permute-start) | collective-permute-done | bytes 131104 | tf_op jit(solution)/shard_map/while/body/eval_jaxpr/ppermute | solution.py:11
  332.5 10.9 %collective-permute-done = f32[32,2,512]{2,1,0:T(2,128)S(1)} collective-permute-done((f32[32,2,512]{2,1,0:T(2,128)S(1)}, f32[32,2,512]{2,1,0:T(2,128)S(1)}, u32[]{:S(2)}, u32[]{:S(2)}) %collective-permute-start) | collective-permute-done | bytes 131104 | tf_op jit(solution)/shard_map/while/body/eval_jaxpr/ppermute | solution.py:11
  346.4 10.9 %collective-permute-done = f32[32,2,512]{2,1,0:T(2,128)S(1)} collective-permute-done((f32[32,2,512]{2,1,0:T(2,128)S(1)}, f32[32,2,512]{2,1,0:T(2,128)S(1)}, u32[]{:S(2)}, u32[]{:S(2)}) %collective-permute-start) | collective-permute-done | bytes 131104 | tf_op jit(solution)/shard_map/while/body/eval_jaxpr/ppermute | solution.py:11
  360.3 10.9 %collective-permute-done = f32[32,2,512]{2,1,0:T(2,128)S(1)} collective-permute-done((f32[32,2,512]{2,1,0:T(2,128)S(1)}, f32[32,2,512]{2,1,0:T(2,128)S(1)}, u32[]{:S(2)}, u32[]{:S(2)}) %collective-permute-start) | collective-permute-done | bytes 131104 | tf_op jit(solution)/shard_map/while/body/eval_jaxpr/ppermute | solution.py:11
  374.2 10.9 %collective-permute-done = f32[32,2,512]{2,1,0:T(2,128)S(1)} collective-permute-done((f32[32,2,512]{2,1,0:T(2,128)S(1)}, f32[32,2,512]{2,1,0:T(2,128)S(1)}, u32[]{:S(2)}, u32[]{:S(2)}) %collective-permute-start) | collective-permute-done | bytes 131104 | tf_op jit(solution)/shard_map/while/body/eval_jaxpr/ppermute | solution.py:11
  388.0 10.9 %collective-permute-done = f32[32,2,512]{2,1,0:T(2,128)S(1)} collective-permute-done((f32[32,2,512]{2,1,0:T(2,128)S(1)}, f32[32,2,512]{2,1,0:T(2,128)S(1)}, u32[]{:S(2)}, u32[]{:S(2)}) %collective-permute-start) | collective-permute-done | bytes 131104 | tf_op jit(solution)/shard_map/while/body/eval_jaxpr/ppermute | solution.py:11
  401.9 10.9 %collective-permute-done = f32[32,2,512]{2,1,0:T(2,128)S(1)} collective-permute-done((f32[32,2,512]{2,1,0:T(2,128)S(1)}, f32[32,2,512]{2,1,0:T(2,128)S(1)}, u32[]{:S(2)}, u32[]{:S(2)}) %collective-permute-start) | collective-permute-done | bytes 131104 | tf_op jit(solution)/shard_map/while/body/eval_jaxpr/ppermute | solution.py:11
  415.8 10.9 %collective-permute-done = f32[32,2,512]{2,1,0:T(2,128)S(1)} collective-permute-done((f32[32,2,512]{2,1,0:T(2,128)S(1)}, f32[32,2,512]{2,1,0:T(2,128)S(1)}, u32[]{:S(2)}, u32[]{:S(2)}) %collective-permute-start) | collective-permute-done | bytes 131104 | tf_op jit(solution)/shard_map/while/body/eval_jaxpr/ppermute | solution.py:11
  429.7 10.9 %collective-permute-done = f32[32,2,512]{2,1,0:T(2,128)S(1)} collective-permute-done((f32[32,2,512]{2,1,0:T(2,128)S(1)}, f32[32,2,512]{2,1,0:T(2,128)S(1)}, u32[]{:S(2)}, u32[]{:S(2)}) %collective-permute-start) | collective-permute-done | bytes 131104 | tf_op jit(solution)/shard_map/while/body/eval_jaxpr/ppermute | solution.py:11
  443.5 10.9 %collective-permute-done = f32[32,2,512]{2,1,0:T(2,128)S(1)} collective-permute-done((f32[32,2,512]{2,1,0:T(2,128)S(1)}, f32[32,2,512]{2,1,0:T(2,128)S(1)}, u32[]{:S(2)}, u32[]{:S(2)}) %collective-permute-start) | collective-permute-done | bytes 131104 | tf_op jit(solution)/shard_map/while/body/eval_jaxpr/ppermute | solution.py:11
  457.4 10.9 %collective-permute-done = f32[32,2,512]{2,1,0:T(2,128)S(1)} collective-permute-done((f32[32,2,512]{2,1,0:T(2,128)S(1)}, f32[32,2,512]{2,1,0:T(2,128)S(1)}, u32[]{:S(2)}, u32[]{:S(2)}) %collective-permute-start) | collective-permute-done | bytes 131104 | tf_op jit(solution)/shard_map/while/body/eval_jaxpr/ppermute | solution.py:11
  471.3 10.9 %collective-permute-done = f32[32,2,512]{2,1,0:T(2,128)S(1)} collective-permute-done((f32[32,2,512]{2,1,0:T(2,128)S(1)}, f32[32,2,512]{2,1,0:T(2,128)S(1)}, u32[]{:S(2)}, u32[]{:S(2)}) %collective-permute-start) | collective-permute-done | bytes 131104 | tf_op jit(solution)/shard_map/while/body/eval_jaxpr/ppermute | solution.py:11
  (75 shorter events, 57.8 us)
Async XLA Ops:
  6.5 121.5 %all-gather.7.cloned.1.call-start = ((), (), s32[]{:S(2)}) async-start(), calls=%async_computation.1 | async-start | bytes 1081344 | tf_op jit(solution)/shard_map/all_gather | solution.py:38
  8.0 226.4 %all-gather.5.cloned.1.call-start = ((), (), s32[]{:S(2)}) async-start(), calls=%async_computation | async-start | bytes 1081344 | tf_op jit(solution)/shard_map/all_gather | solution.py:38
  8.8 2.9 copy-start.9
  8.8 2.9 copy-start.5
  15.2 1.3 copy-start.3
  130.4 105.6 %copy-start.7 = (bf16[64,8,2,512]{3,1,2,0:T(8,128)(2,1)S(1)}, bf16[64,8,2,512]{3,1,2,0:T(8,128)(2,1)}, u32[]{:S(2)}) copy-start(bf16[64,8,2,512]{3,1,2,0:T(8,128)(2,1)} %copy.20) | copy-start | bytes 3145732
  234.4 1.5 copy-start.4
  237.3 1.6 copy-start.6
  247.6 4.2 copy-start
  256.1 3.2 copy-start.1
  256.1 3.2 copy-start.2
  275.1 12.9 %collective-permute-start = (f32[32,2,512]{2,1,0:T(2,128)S(1)}, f32[32,2,512]{2,1,0:T(2,128)S(1)}, u32[]{:S(2)}, u32[]{:S(2)}) collective-permute-start(f32[32,2,512]{2,1,0:T(2,128)S(1)} %get-tuple-element.188), channel_id=1, source_target_pairs={{0,32},{32,64},{64,96},{96,128},{128,160},{160,192},{192,224},{224... | collective-permute-start | bytes 393224 | tf_op jit(solution)/shard_map/while/body/eval_jaxpr/ppermute | solution.py:11
  288.9 12.9 %collective-permute-start = (f32[32,2,512]{2,1,0:T(2,128)S(1)}, f32[32,2,512]{2,1,0:T(2,128)S(1)}, u32[]{:S(2)}, u32[]{:S(2)}) collective-permute-start(f32[32,2,512]{2,1,0:T(2,128)S(1)} %get-tuple-element.188), channel_id=1, source_target_pairs={{0,32},{32,64},{64,96},{96,128},{128,160},{160,192},{192,224},{224... | collective-permute-start | bytes 393224 | tf_op jit(solution)/shard_map/while/body/eval_jaxpr/ppermute | solution.py:11
  302.8 12.9 %collective-permute-start = (f32[32,2,512]{2,1,0:T(2,128)S(1)}, f32[32,2,512]{2,1,0:T(2,128)S(1)}, u32[]{:S(2)}, u32[]{:S(2)}) collective-permute-start(f32[32,2,512]{2,1,0:T(2,128)S(1)} %get-tuple-element.188), channel_id=1, source_target_pairs={{0,32},{32,64},{64,96},{96,128},{128,160},{160,192},{192,224},{224... | collective-permute-start | bytes 393224 | tf_op jit(solution)/shard_map/while/body/eval_jaxpr/ppermute | solution.py:11
  316.7 12.9 %collective-permute-start = (f32[32,2,512]{2,1,0:T(2,128)S(1)}, f32[32,2,512]{2,1,0:T(2,128)S(1)}, u32[]{:S(2)}, u32[]{:S(2)}) collective-permute-start(f32[32,2,512]{2,1,0:T(2,128)S(1)} %get-tuple-element.188), channel_id=1, source_target_pairs={{0,32},{32,64},{64,96},{96,128},{128,160},{160,192},{192,224},{224... | collective-permute-start | bytes 393224 | tf_op jit(solution)/shard_map/while/body/eval_jaxpr/ppermute | solution.py:11
  330.6 12.9 %collective-permute-start = (f32[32,2,512]{2,1,0:T(2,128)S(1)}, f32[32,2,512]{2,1,0:T(2,128)S(1)}, u32[]{:S(2)}, u32[]{:S(2)}) collective-permute-start(f32[32,2,512]{2,1,0:T(2,128)S(1)} %get-tuple-element.188), channel_id=1, source_target_pairs={{0,32},{32,64},{64,96},{96,128},{128,160},{160,192},{192,224},{224... | collective-permute-start | bytes 393224 | tf_op jit(solution)/shard_map/while/body/eval_jaxpr/ppermute | solution.py:11
  344.4 12.9 %collective-permute-start = (f32[32,2,512]{2,1,0:T(2,128)S(1)}, f32[32,2,512]{2,1,0:T(2,128)S(1)}, u32[]{:S(2)}, u32[]{:S(2)}) collective-permute-start(f32[32,2,512]{2,1,0:T(2,128)S(1)} %get-tuple-element.188), channel_id=1, source_target_pairs={{0,32},{32,64},{64,96},{96,128},{128,160},{160,192},{192,224},{224... | collective-permute-start | bytes 393224 | tf_op jit(solution)/shard_map/while/body/eval_jaxpr/ppermute | solution.py:11
  358.3 12.9 %collective-permute-start = (f32[32,2,512]{2,1,0:T(2,128)S(1)}, f32[32,2,512]{2,1,0:T(2,128)S(1)}, u32[]{:S(2)}, u32[]{:S(2)}) collective-permute-start(f32[32,2,512]{2,1,0:T(2,128)S(1)} %get-tuple-element.188), channel_id=1, source_target_pairs={{0,32},{32,64},{64,96},{96,128},{128,160},{160,192},{192,224},{224... | collective-permute-start | bytes 393224 | tf_op jit(solution)/shard_map/while/body/eval_jaxpr/ppermute | solution.py:11
  372.2 12.9 %collective-permute-start = (f32[32,2,512]{2,1,0:T(2,128)S(1)}, f32[32,2,512]{2,1,0:T(2,128)S(1)}, u32[]{:S(2)}, u32[]{:S(2)}) collective-permute-start(f32[32,2,512]{2,1,0:T(2,128)S(1)} %get-tuple-element.188), channel_id=1, source_target_pairs={{0,32},{32,64},{64,96},{96,128},{128,160},{160,192},{192,224},{224... | collective-permute-start | bytes 393224 | tf_op jit(solution)/shard_map/while/body/eval_jaxpr/ppermute | solution.py:11
  386.1 12.9 %collective-permute-start = (f32[32,2,512]{2,1,0:T(2,128)S(1)}, f32[32,2,512]{2,1,0:T(2,128)S(1)}, u32[]{:S(2)}, u32[]{:S(2)}) collective-permute-start(f32[32,2,512]{2,1,0:T(2,128)S(1)} %get-tuple-element.188), channel_id=1, source_target_pairs={{0,32},{32,64},{64,96},{96,128},{128,160},{160,192},{192,224},{224... | collective-permute-start | bytes 393224 | tf_op jit(solution)/shard_map/while/body/eval_jaxpr/ppermute | solution.py:11
  400.0 12.9 %collective-permute-start = (f32[32,2,512]{2,1,0:T(2,128)S(1)}, f32[32,2,512]{2,1,0:T(2,128)S(1)}, u32[]{:S(2)}, u32[]{:S(2)}) collective-permute-start(f32[32,2,512]{2,1,0:T(2,128)S(1)} %get-tuple-element.188), channel_id=1, source_target_pairs={{0,32},{32,64},{64,96},{96,128},{128,160},{160,192},{192,224},{224... | collective-permute-start | bytes 393224 | tf_op jit(solution)/shard_map/while/body/eval_jaxpr/ppermute | solution.py:11
  413.8 12.9 %collective-permute-start = (f32[32,2,512]{2,1,0:T(2,128)S(1)}, f32[32,2,512]{2,1,0:T(2,128)S(1)}, u32[]{:S(2)}, u32[]{:S(2)}) collective-permute-start(f32[32,2,512]{2,1,0:T(2,128)S(1)} %get-tuple-element.188), channel_id=1, source_target_pairs={{0,32},{32,64},{64,96},{96,128},{128,160},{160,192},{192,224},{224... | collective-permute-start | bytes 393224 | tf_op jit(solution)/shard_map/while/body/eval_jaxpr/ppermute | solution.py:11
  427.7 12.9 %collective-permute-start = (f32[32,2,512]{2,1,0:T(2,128)S(1)}, f32[32,2,512]{2,1,0:T(2,128)S(1)}, u32[]{:S(2)}, u32[]{:S(2)}) collective-permute-start(f32[32,2,512]{2,1,0:T(2,128)S(1)} %get-tuple-element.188), channel_id=1, source_target_pairs={{0,32},{32,64},{64,96},{96,128},{128,160},{160,192},{192,224},{224... | collective-permute-start | bytes 393224 | tf_op jit(solution)/shard_map/while/body/eval_jaxpr/ppermute | solution.py:11
  441.6 12.9 %collective-permute-start = (f32[32,2,512]{2,1,0:T(2,128)S(1)}, f32[32,2,512]{2,1,0:T(2,128)S(1)}, u32[]{:S(2)}, u32[]{:S(2)}) collective-permute-start(f32[32,2,512]{2,1,0:T(2,128)S(1)} %get-tuple-element.188), channel_id=1, source_target_pairs={{0,32},{32,64},{64,96},{96,128},{128,160},{160,192},{192,224},{224... | collective-permute-start | bytes 393224 | tf_op jit(solution)/shard_map/while/body/eval_jaxpr/ppermute | solution.py:11
  455.5 12.9 %collective-permute-start = (f32[32,2,512]{2,1,0:T(2,128)S(1)}, f32[32,2,512]{2,1,0:T(2,128)S(1)}, u32[]{:S(2)}, u32[]{:S(2)}) collective-permute-start(f32[32,2,512]{2,1,0:T(2,128)S(1)} %get-tuple-element.188), channel_id=1, source_target_pairs={{0,32},{32,64},{64,96},{96,128},{128,160},{160,192},{192,224},{224... | collective-permute-start | bytes 393224 | tf_op jit(solution)/shard_map/while/body/eval_jaxpr/ppermute | solution.py:11
  469.3 12.9 %collective-permute-start = (f32[32,2,512]{2,1,0:T(2,128)S(1)}, f32[32,2,512]{2,1,0:T(2,128)S(1)}, u32[]{:S(2)}, u32[]{:S(2)}) collective-permute-start(f32[32,2,512]{2,1,0:T(2,128)S(1)} %get-tuple-element.188), channel_id=1, source_target_pairs={{0,32},{32,64},{64,96},{96,128},{128,160},{160,192},{192,224},{224... | collective-permute-start | bytes 393224 | tf_op jit(solution)/shard_map/while/body/eval_jaxpr/ppermute | solution.py:11
  483.2 0.7 copy-start.8
Sparse Core Ops, SparseCore 0:
  11.8 116.2 all-gather.6
  132.5 101.9 all-gather.4
where the time goes:
time: 492 us; the launch traced here: 491 us
  waiting for transfers between devices  371 us (75%)
  other arithmetic  38 us (8%)
  local copies, waits for them, and re-layouts  35.6 us (7%)
  starting transfers between devices  28.9 us (6%)
  between operations  13.7 us (3%)
    all_gather x2, waiting for transfers between devices, body(): lax.all_gather(branch_tensor[slice_pos], 'stem', axis=0, tiled=True)  207 us
    ppermute x15, waiting for transfers between devices, from_behind(): return lax.ppermute(value, axis, pairs)  164 us
    ppermute x15, starting transfers between devices, from_behind(): return lax.ppermute(value, axis, pairs)  28.8 us
    add x15, other arithmetic, pass_along(): return from_behind(running, 'cuts', 1) + pick_block(turn)  14.6 us
  transfers between devices with their start and end apart: 17, of which 17 were waited for; matrix products, arithmetic and copies ran while one was open for 4% of the time, Pallas kernels for 0%

commit v1 on v0

--- a/solution.py
+++ b/solution.py
@@ -3,6 +3,11 @@
 import jax.numpy as jnp
 from jax import lax
 from jax.sharding import PartitionSpec as P
+
+bring_the_pieces_all = lambda point, axis_tag: jnp.concatenate(
+    lax.all_to_all(jnp.stack([point for _ in range(lax.axis_size(axis_tag))]), axis_tag, 0, 0),
+    axis=0,
+)
 
 
 def from_behind(value, axis, steps):
@@ -33,11 +38,7 @@
         initial = jnp.zeros((row_count, 2, width), jnp.float32)
         folder = partial(fold_rows, stem_tensor[slice_pos])
         image_list.append(
-            folder(
-                initial,
-                lax.all_gather(branch_tensor[slice_pos], "stem", axis=0, tiled=True),
-                jnp.int32(0),
-            )
+            folder(initial, bring_the_pieces_all(branch_tensor[slice_pos], "stem"), jnp.int32(0))
         )
     local_sum = jnp.zeros((row_count, 2, width), jnp.float32)
     for slice_pos in range(slice_count):

time: 492 us -> 359 us (0.73)
  the two profiles are of different devices: /device:TPU:2 before, /device:TPU:8 now
where the time goes in v1:
time: 359 us; the launch traced here: 358 us
  waiting for transfers between devices  193 us (54%)
  starting transfers between devices  87.7 us (24%)
  local copies, waits for them, and re-layouts  37.5 us (10%)
  other arithmetic  36.8 us (10%)
    ppermute x15, waiting for transfers between devices, from_behind(): return lax.ppermute(value, axis, pairs)  151 us
    ppermute x15, starting transfers between devices, from_behind(): return lax.ppermute(value, axis, pairs)  61.7 us
    all_to_all x2, waiting for transfers between devices, lax.all_to_all(jnp.stack([point for _ in range(lax.axis_size(axis_tag))])...  41.9 us
    all_to_all x2, starting transfers between devices, lax.all_to_all(jnp.stack([point for _ in range(lax.axis_size(axis_tag))])...  25.9 us
    add x15, other arithmetic, pass_along(): return from_behind(running, 'cuts', 1) + pick_block(turn)  14.6 us
    unnamed x22, local copies, waits for them, and re-layouts  11.1 us
    gather x2, local copies, waits for them, and re-layouts, body(): placed = jnp.take(image_list[slice_pos], open_order[slice_pos], axis=2)  8.68 us
    select_n x4, other arithmetic, body(): placed = jnp.take(image_list[slice_pos], open_order[slice_pos], axis=2)  7.35 us
  transfers between devices with their start and end apart: 17, of which 17 were waited for; matrix products, arithmetic and copies ran while one was open for 5% of the time, Pallas kernels for 0%

profile of v1, /device:TPU:8, one launch (start us, length us, event | category | flops | bytes accessed | tf_op | source)
XLA Modules:
  0.0 358.2 jit_solution(11829776152661926602)
XLA Ops:
  2.0 20.8 %all-to-all-start = ((bf16[32,16,2,512]{3,1,2,0:T(8,128)(2,1)}), bf16[32,16,2,512]{3,1,2,0:T(8,128)(2,1)S(1)}, u32[]{:S(2)}, u32[]{:S(2)}) async-start(bf16[32,16,2,512]{3,1,2,0:T(8,128)(2,1)} %stack.16), calls=%async_computation | async-start | bytes 2097152 | tf_op jit(solution)/shard_map/all_to_all | solution.py:8
  22.8 29.7 %all-to-all-done = bf16[32,16,2,512]{3,1,2,0:T(8,128)(2,1)S(1)} async-done(((bf16[32,16,2,512]{3,1,2,0:T(8,128)(2,1)}), bf16[32,16,2,512]{3,1,2,0:T(8,128)(2,1)S(1)}, u32[]{:S(2)}, u32[]{:S(2)}) %all-to-all-start) | async-done | bytes 1048608 | tf_op jit(solution)/shard_map/all_to_all | solution.py:8
  53.6 5.1 %all-to-all-start.1 = ((bf16[32,16,2,512]{3,1,2,0:T(8,128)(2,1)}), bf16[32,16,2,512]{3,1,2,0:T(8,128)(2,1)}, u32[]{:S(2)}, u32[]{:S(2)}) async-start(bf16[32,16,2,512]{3,1,2,0:T(8,128)(2,1)} %stack.18), calls=%async_computation.1 | async-start | bytes 2097152 | tf_op jit(solution)/shard_map/all_to_all | solution.py:8
  62.8 2.2 fusion.21
  65.0 2.1 copy.26
  67.1 4.7 %copy.25 = bf16[1,512,2,512]{1,2,3,0:T(2,128)(2,1)S(1)} copy(bf16[1,512,2,512]{3,2,1,0:T(2,128)(2,1)} %get-tuple-element.145) | data formatting | bytes 2097152
  76.2 12.2 %all-to-all-done.1 = bf16[32,16,2,512]{3,1,2,0:T(8,128)(2,1)} async-done(((bf16[32,16,2,512]{3,1,2,0:T(8,128)(2,1)}), bf16[32,16,2,512]{3,1,2,0:T(8,128)(2,1)}, u32[]{:S(2)}, u32[]{:S(2)}) %all-to-all-start.1) | async-done | bytes 1048608 | tf_op jit(solution)/shard_map/all_to_all | solution.py:8
  95.2 3.0 copy.21
  98.2 4.4 %gather_fusion = f32[512,512,2]{1,2,0:T(2,128)} fusion(f32[512,2,512]{0,1,2:T(2,128)S(1)} %copy.17, s32[1024]{0:T(1024)S(1)} %pad_clamp_fusion.1), kind=kCustom, calls=%fused_computation.clone | custom fusion | bytes 4196352 | tf_op jit(solution)/shard_map/jit(_take)/gather | solution.py:45
  102.6 4.2 %select_bitcast_fusion.1 = f32[512,2,512]{0,1,2:T(2,128)} fusion(f32[512,512,2]{1,2,0:T(2,128)} %gather_fusion, pred[512]{0:T(512)(128)(4,1)S(1)} %compare_and_fusion.1), kind=kLoop, calls=%fused_computation.21 | loop fusion | flops 524288 | bytes 4194816 | tf_op jit(solution)/shard_map/jit(_take)/select_n | solution.py:45
  106.7 4.3 %gather_fusion.1 = f32[512,512,2]{1,2,0:T(2,128)} fusion(f32[512,2,512]{0,1,2:T(2,128)S(1)} %copy-done, s32[1024]{0:T(1024)S(1)} %pad_clamp_fusion), kind=kCustom, calls=%fused_computation.1.clone | custom fusion | bytes 4196352 | tf_op jit(solution)/shard_map/jit(_take)/gather | solution.py:45
  111.1 3.2 select_bitcast_fusion
  114.2 7.2 %multiply_subtract_fusion = (f32[512,1,512]{0,1,2:T(1,128)S(1)}, f32[512,1,512]{0,1,2:T(1,128)S(1)}, f32[512,1,512]{0,1,2:T(1,128)S(1)}, f32[512,1,512]{0,1,2:T(1,128)S(1)}) fusion(f32[512,2,512]{0,1,2:T(2,128)S(1)} %copy-done.1, f32[512,2,512]{0,1,2:T(2,128)S(1)} %select_bitcast_fusion, f32[512,2,512]{0,1,2:T(2,128)S(1)} %copy-done.2, ...), kind=kLoop, calls=%fused_computation.25 | loop fusion | flops 3145728 | bytes 12582912 | tf_op jit(solution)/shard_map/sub | solution.py:47
  121.4 3.5 maximum_add_fusion
  124.9 4.1 %copy.24 = f32[512,2,512]{2,1,0:T(2,128)} copy(f32[512,2,512]{0,1,2:T(2,128)S(1)} %maximum_add_fusion) | data formatting | bytes 4194304 | tf_op jit(solution)/shard_map/while | solution.py:61
  129.8 227.7 %while.15 = (s32[]{:T(128)}, f32[32,2,512]{2,1,0:T(2,128)S(1)}, s32[]{:T(128)}, f32[512,2,512]{2,1,0:T(2,128)}, s32[]{:T(128)}, /*index=5*/s32[]{:T(128)}, s32[]{:T(128)}, s32[]{:T(128)}, s32[]{:T(128)}, s32[]{:T(128)}) while((s32[]{:T(128)}, f32[32,2,512]{2,1,0:T(2,128)S(1)}, s32[]{:T(128)}, f32[512,2,512]{2,1,0:T(2,128)}, s32[]{:T(128)}, ...), condition=%wide.region_1.3_spmd, body=%wide.region_0.0_spmd.sunk | while | flops 32786 | bytes 917816 | solution.py:61
  131.8 10.9 %collective-permute-done = f32[32,2,512]{2,1,0:T(2,128)S(1)} collective-permute-done((f32[32,2,512]{2,1,0:T(2,128)S(1)}, f32[32,2,512]{2,1,0:T(2,128)S(1)}, u32[]{:S(2)}, u32[]{:S(2)}) %collective-permute-start) | collective-permute-done | bytes 131104 | tf_op jit(solution)/shard_map/while/body/eval_jaxpr/ppermute | solution.py:16
  143.7 31.5 %collective-permute-start = (f32[32,2,512]{2,1,0:T(2,128)S(1)}, f32[32,2,512]{2,1,0:T(2,128)S(1)}, u32[]{:S(2)}, u32[]{:S(2)}) collective-permute-start(f32[32,2,512]{2,1,0:T(2,128)S(1)} %get-tuple-element.192), channel_id=1, source_target_pairs={{0,32},{32,64},{64,96},{96,128},{128,160},{160,192},{192,224},{224... | collective-permute-start | bytes 393224 | tf_op jit(solution)/shard_map/while/body/eval_jaxpr/ppermute | solution.py:16
  177.1 5.3 %collective-permute-start = (f32[32,2,512]{2,1,0:T(2,128)S(1)}, f32[32,2,512]{2,1,0:T(2,128)S(1)}, u32[]{:S(2)}, u32[]{:S(2)}) collective-permute-start(f32[32,2,512]{2,1,0:T(2,128)S(1)} %get-tuple-element.192), channel_id=1, source_target_pairs={{0,32},{32,64},{64,96},{96,128},{128,160},{160,192},{192,224},{224... | collective-permute-start | bytes 393224 | tf_op jit(solution)/shard_map/while/body/eval_jaxpr/ppermute | solution.py:16
  182.4 7.5 %collective-permute-done = f32[32,2,512]{2,1,0:T(2,128)S(1)} collective-permute-done((f32[32,2,512]{2,1,0:T(2,128)S(1)}, f32[32,2,512]{2,1,0:T(2,128)S(1)}, u32[]{:S(2)}, u32[]{:S(2)}) %collective-permute-start) | collective-permute-done | bytes 131104 | tf_op jit(solution)/shard_map/while/body/eval_jaxpr/ppermute | solution.py:16
  192.9 10.9 %collective-permute-done = f32[32,2,512]{2,1,0:T(2,128)S(1)} collective-permute-done((f32[32,2,512]{2,1,0:T(2,128)S(1)}, f32[32,2,512]{2,1,0:T(2,128)S(1)}, u32[]{:S(2)}, u32[]{:S(2)}) %collective-permute-start) | collective-permute-done | bytes 131104 | tf_op jit(solution)/shard_map/while/body/eval_jaxpr/ppermute | solution.py:16
  206.8 10.9 %collective-permute-done = f32[32,2,512]{2,1,0:T(2,128)S(1)} collective-permute-done((f32[32,2,512]{2,1,0:T(2,128)S(1)}, f32[32,2,512]{2,1,0:T(2,128)S(1)}, u32[]{:S(2)}, u32[]{:S(2)}) %collective-permute-start) | collective-permute-done | bytes 131104 | tf_op jit(solution)/shard_map/while/body/eval_jaxpr/ppermute | solution.py:16
  220.7 10.9 %collective-permute-done = f32[32,2,512]{2,1,0:T(2,128)S(1)} collective-permute-done((f32[32,2,512]{2,1,0:T(2,128)S(1)}, f32[32,2,512]{2,1,0:T(2,128)S(1)}, u32[]{:S(2)}, u32[]{:S(2)}) %collective-permute-start) | collective-permute-done | bytes 131104 | tf_op jit(solution)/shard_map/while/body/eval_jaxpr/ppermute | solution.py:16
  234.6 10.9 %collective-permute-done = f32[32,2,512]{2,1,0:T(2,128)S(1)} collective-permute-done((f32[32,2,512]{2,1,0:T(2,128)S(1)}, f32[32,2,512]{2,1,0:T(2,128)S(1)}, u32[]{:S(2)}, u32[]{:S(2)}) %collective-permute-start) | collective-permute-done | bytes 131104 | tf_op jit(solution)/shard_map/while/body/eval_jaxpr/ppermute | solution.py:16
  248.4 10.9 %collective-permute-done = f32[32,2,512]{2,1,0:T(2,128)S(1)} collective-permute-done((f32[32,2,512]{2,1,0:T(2,128)S(1)}, f32[32,2,512]{2,1,0:T(2,128)S(1)}, u32[]{:S(2)}, u32[]{:S(2)}) %collective-permute-start) | collective-permute-done | bytes 131104 | tf_op jit(solution)/shard_map/while/body/eval_jaxpr/ppermute | solution.py:16
  262.3 10.9 %collective-permute-done = f32[32,2,512]{2,1,0:T(2,128)S(1)} collective-permute-done((f32[32,2,512]{2,1,0:T(2,128)S(1)}, f32[32,2,512]{2,1,0:T(2,128)S(1)}, u32[]{:S(2)}, u32[]{:S(2)}) %collective-permute-start) | collective-permute-done | bytes 131104 | tf_op jit(solution)/shard_map/while/body/eval_jaxpr/ppermute | solution.py:16
  276.2 10.9 %collective-permute-done = f32[32,2,512]{2,1,0:T(2,128)S(1)} collective-permute-done((f32[32,2,512]{2,1,0:T(2,128)S(1)}, f32[32,2,512]{2,1,0:T(2,128)S(1)}, u32[]{:S(2)}, u32[]{:S(2)}) %collective-permute-start) | collective-permute-done | bytes 131104 | tf_op jit(solution)/shard_map/while/body/eval_jaxpr/ppermute | solution.py:16
  290.1 10.9 %collective-permute-done = f32[32,2,512]{2,1,0:T(2,128)S(1)} collective-permute-done((f32[32,2,512]{2,1,0:T(2,128)S(1)}, f32[32,2,512]{2,1,0:T(2,128)S(1)}, u32[]{:S(2)}, u32[]{:S(2)}) %collective-permute-start) | collective-permute-done | bytes 131104 | tf_op jit(solution)/shard_map/while/body/eval_jaxpr/ppermute | solution.py:16
  304.0 10.9 %collective-permute-done = f32[32,2,512]{2,1,0:T(2,128)S(1)} collective-permute-done((f32[32,2,512]{2,1,0:T(2,128)S(1)}, f32[32,2,512]{2,1,0:T(2,128)S(1)}, u32[]{:S(2)}, u32[]{:S(2)}) %collective-permute-start) | collective-permute-done | bytes 131104 | tf_op jit(solution)/shard_map/while/body/eval_jaxpr/ppermute | solution.py:16
  317.8 10.9 %collective-permute-done = f32[32,2,512]{2,1,0:T(2,128)S(1)} collective-permute-done((f32[32,2,512]{2,1,0:T(2,128)S(1)}, f32[32,2,512]{2,1,0:T(2,128)S(1)}, u32[]{:S(2)}, u32[]{:S(2)}) %collective-permute-start) | collective-permute-done | bytes 131104 | tf_op jit(solution)/shard_map/while/body/eval_jaxpr/ppermute | solution.py:16
  331.7 10.9 %collective-permute-done = f32[32,2,512]{2,1,0:T(2,128)S(1)} collective-permute-done((f32[32,2,512]{2,1,0:T(2,128)S(1)}, f32[32,2,512]{2,1,0:T(2,128)S(1)}, u32[]{:S(2)}, u32[]{:S(2)}) %collective-permute-start) | collective-permute-done | bytes 131104 | tf_op jit(solution)/shard_map/while/body/eval_jaxpr/ppermute | solution.py:16
  345.6 10.9 %collective-permute-done = f32[32,2,512]{2,1,0:T(2,128)S(1)} collective-permute-done((f32[32,2,512]{2,1,0:T(2,128)S(1)}, f32[32,2,512]{2,1,0:T(2,128)S(1)}, u32[]{:S(2)}, u32[]{:S(2)}) %collective-permute-start) | collective-permute-done | bytes 131104 | tf_op jit(solution)/shard_map/while/body/eval_jaxpr/ppermute | solution.py:16
  (75 shorter events, 60.1 us)
Async XLA Ops:
  2.0 50.5 %all-to-all-start = ((bf16[32,16,2,512]{3,1,2,0:T(8,128)(2,1)}), bf16[32,16,2,512]{3,1,2,0:T(8,128)(2,1)S(1)}, u32[]{:S(2)}, u32[]{:S(2)}) async-start(bf16[32,16,2,512]{3,1,2,0:T(8,128)(2,1)} %stack.16), calls=%async_computation | async-start | bytes 2097152 | tf_op jit(solution)/shard_map/all_to_all | solution.py:8
  22.7 36.0 %copy-start.3 = (bf16[2,512,2,512]{3,2,1,0:T(2,128)(2,1)S(1)}, bf16[2,512,2,512]{3,2,1,0:T(2,128)(2,1)}, u32[]{:S(2)}) copy-start(bf16[2,512,2,512]{3,2,1,0:T(2,128)(2,1)} %param.8) | copy-start | bytes 6291460
  53.6 34.9 %all-to-all-start.1 = ((bf16[32,16,2,512]{3,1,2,0:T(8,128)(2,1)}), bf16[32,16,2,512]{3,1,2,0:T(8,128)(2,1)}, u32[]{:S(2)}, u32[]{:S(2)}) async-start(bf16[32,16,2,512]{3,1,2,0:T(8,128)(2,1)} %stack.18), calls=%async_computation.1 | async-start | bytes 2097152 | tf_op jit(solution)/shard_map/all_to_all | solution.py:8
  60.2 2.5 copy-start.4
  65.0 6.8 %copy-start.8 = (s32[2,512]{1,0:T(2,128)S(1)}, s32[2,512]{1,0:T(2,128)}, u32[]{:S(2)}) copy-start(s32[2,512]{1,0:T(2,128)} %param.11) | copy-start | bytes 12292
  89.7 1.2 copy-start.6
  92.3 1.6 copy-start.5
  102.6 4.2 %copy-start = (f32[512,2,512]{0,1,2:T(2,128)S(1)}, f32[512,2,512]{0,1,2:T(2,128)}, u32[]{:S(2)}) copy-start(f32[512,2,512]{0,1,2:T(2,128)} %copy.21) | copy-start | bytes 6291460
  111.0 3.2 copy-start.1
  111.1 3.2 copy-start.2
  129.8 12.9 %collective-permute-start = (f32[32,2,512]{2,1,0:T(2,128)S(1)}, f32[32,2,512]{2,1,0:T(2,128)S(1)}, u32[]{:S(2)}, u32[]{:S(2)}) collective-permute-start(f32[32,2,512]{2,1,0:T(2,128)S(1)} %get-tuple-element.192), channel_id=1, source_target_pairs={{0,32},{32,64},{64,96},{96,128},{128,160},{160,192},{192,224},{224... | collective-permute-start | bytes 393224 | tf_op jit(solution)/shard_map/while/body/eval_jaxpr/ppermute | solution.py:16
  143.7 32.4 %collective-permute-start = (f32[32,2,512]{2,1,0:T(2,128)S(1)}, f32[32,2,512]{2,1,0:T(2,128)S(1)}, u32[]{:S(2)}, u32[]{:S(2)}) collective-permute-start(f32[32,2,512]{2,1,0:T(2,128)S(1)} %get-tuple-element.192), channel_id=1, source_target_pairs={{0,32},{32,64},{64,96},{96,128},{128,160},{160,192},{192,224},{224... | collective-permute-start | bytes 393224 | tf_op jit(solution)/shard_map/while/body/eval_jaxpr/ppermute | solution.py:16
  177.1 12.9 %collective-permute-start = (f32[32,2,512]{2,1,0:T(2,128)S(1)}, f32[32,2,512]{2,1,0:T(2,128)S(1)}, u32[]{:S(2)}, u32[]{:S(2)}) collective-permute-start(f32[32,2,512]{2,1,0:T(2,128)S(1)} %get-tuple-element.192), channel_id=1, source_target_pairs={{0,32},{32,64},{64,96},{96,128},{128,160},{160,192},{192,224},{224... | collective-permute-start | bytes 393224 | tf_op jit(solution)/shard_map/while/body/eval_jaxpr/ppermute | solution.py:16
  191.0 12.9 %collective-permute-start = (f32[32,2,512]{2,1,0:T(2,128)S(1)}, f32[32,2,512]{2,1,0:T(2,128)S(1)}, u32[]{:S(2)}, u32[]{:S(2)}) collective-permute-start(f32[32,2,512]{2,1,0:T(2,128)S(1)} %get-tuple-element.192), channel_id=1, source_target_pairs={{0,32},{32,64},{64,96},{96,128},{128,160},{160,192},{192,224},{224... | collective-permute-start | bytes 393224 | tf_op jit(solution)/shard_map/while/body/eval_jaxpr/ppermute | solution.py:16
  204.9 12.9 %collective-permute-start = (f32[32,2,512]{2,1,0:T(2,128)S(1)}, f32[32,2,512]{2,1,0:T(2,128)S(1)}, u32[]{:S(2)}, u32[]{:S(2)}) collective-permute-start(f32[32,2,512]{2,1,0:T(2,128)S(1)} %get-tuple-element.192), channel_id=1, source_target_pairs={{0,32},{32,64},{64,96},{96,128},{128,160},{160,192},{192,224},{224... | collective-permute-start | bytes 393224 | tf_op jit(solution)/shard_map/while/body/eval_jaxpr/ppermute | solution.py:16
  218.7 12.9 %collective-permute-start = (f32[32,2,512]{2,1,0:T(2,128)S(1)}, f32[32,2,512]{2,1,0:T(2,128)S(1)}, u32[]{:S(2)}, u32[]{:S(2)}) collective-permute-start(f32[32,2,512]{2,1,0:T(2,128)S(1)} %get-tuple-element.192), channel_id=1, source_target_pairs={{0,32},{32,64},{64,96},{96,128},{128,160},{160,192},{192,224},{224... | collective-permute-start | bytes 393224 | tf_op jit(solution)/shard_map/while/body/eval_jaxpr/ppermute | solution.py:16
  232.6 12.9 %collective-permute-start = (f32[32,2,512]{2,1,0:T(2,128)S(1)}, f32[32,2,512]{2,1,0:T(2,128)S(1)}, u32[]{:S(2)}, u32[]{:S(2)}) collective-permute-start(f32[32,2,512]{2,1,0:T(2,128)S(1)} %get-tuple-element.192), channel_id=1, source_target_pairs={{0,32},{32,64},{64,96},{96,128},{128,160},{160,192},{192,224},{224... | collective-permute-start | bytes 393224 | tf_op jit(solution)/shard_map/while/body/eval_jaxpr/ppermute | solution.py:16
  246.5 12.9 %collective-permute-start = (f32[32,2,512]{2,1,0:T(2,128)S(1)}, f32[32,2,512]{2,1,0:T(2,128)S(1)}, u32[]{:S(2)}, u32[]{:S(2)}) collective-permute-start(f32[32,2,512]{2,1,0:T(2,128)S(1)} %get-tuple-element.192), channel_id=1, source_target_pairs={{0,32},{32,64},{64,96},{96,128},{128,160},{160,192},{192,224},{224... | collective-permute-start | bytes 393224 | tf_op jit(solution)/shard_map/while/body/eval_jaxpr/ppermute | solution.py:16
  260.4 12.9 %collective-permute-start = (f32[32,2,512]{2,1,0:T(2,128)S(1)}, f32[32,2,512]{2,1,0:T(2,128)S(1)}, u32[]{:S(2)}, u32[]{:S(2)}) collective-permute-start(f32[32,2,512]{2,1,0:T(2,128)S(1)} %get-tuple-element.192), channel_id=1, source_target_pairs={{0,32},{32,64},{64,96},{96,128},{128,160},{160,192},{192,224},{224... | collective-permute-start | bytes 393224 | tf_op jit(solution)/shard_map/while/body/eval_jaxpr/ppermute | solution.py:16
  274.2 12.9 %collective-permute-start = (f32[32,2,512]{2,1,0:T(2,128)S(1)}, f32[32,2,512]{2,1,0:T(2,128)S(1)}, u32[]{:S(2)}, u32[]{:S(2)}) collective-permute-start(f32[32,2,512]{2,1,0:T(2,128)S(1)} %get-tuple-element.192), channel_id=1, source_target_pairs={{0,32},{32,64},{64,96},{96,128},{128,160},{160,192},{192,224},{224... | collective-permute-start | bytes 393224 | tf_op jit(solution)/shard_map/while/body/eval_jaxpr/ppermute | solution.py:16
  288.1 12.9 %collective-permute-start = (f32[32,2,512]{2,1,0:T(2,128)S(1)}, f32[32,2,512]{2,1,0:T(2,128)S(1)}, u32[]{:S(2)}, u32[]{:S(2)}) collective-permute-start(f32[32,2,512]{2,1,0:T(2,128)S(1)} %get-tuple-element.192), channel_id=1, source_target_pairs={{0,32},{32,64},{64,96},{96,128},{128,160},{160,192},{192,224},{224... | collective-permute-start | bytes 393224 | tf_op jit(solution)/shard_map/while/body/eval_jaxpr/ppermute | solution.py:16
  302.0 12.9 %collective-permute-start = (f32[32,2,512]{2,1,0:T(2,128)S(1)}, f32[32,2,512]{2,1,0:T(2,128)S(1)}, u32[]{:S(2)}, u32[]{:S(2)}) collective-permute-start(f32[32,2,512]{2,1,0:T(2,128)S(1)} %get-tuple-element.192), channel_id=1, source_target_pairs={{0,32},{32,64},{64,96},{96,128},{128,160},{160,192},{192,224},{224... | collective-permute-start | bytes 393224 | tf_op jit(solution)/shard_map/while/body/eval_jaxpr/ppermute | solution.py:16
  315.9 12.9 %collective-permute-start = (f32[32,2,512]{2,1,0:T(2,128)S(1)}, f32[32,2,512]{2,1,0:T(2,128)S(1)}, u32[]{:S(2)}, u32[]{:S(2)}) collective-permute-start(f32[32,2,512]{2,1,0:T(2,128)S(1)} %get-tuple-element.192), channel_id=1, source_target_pairs={{0,32},{32,64},{64,96},{96,128},{128,160},{160,192},{192,224},{224... | collective-permute-start | bytes 393224 | tf_op jit(solution)/shard_map/while/body/eval_jaxpr/ppermute | solution.py:16
  329.8 12.9 %collective-permute-start = (f32[32,2,512]{2,1,0:T(2,128)S(1)}, f32[32,2,512]{2,1,0:T(2,128)S(1)}, u32[]{:S(2)}, u32[]{:S(2)}) collective-permute-start(f32[32,2,512]{2,1,0:T(2,128)S(1)} %get-tuple-element.192), channel_id=1, source_target_pairs={{0,32},{32,64},{64,96},{96,128},{128,160},{160,192},{192,224},{224... | collective-permute-start | bytes 393224 | tf_op jit(solution)/shard_map/while/body/eval_jaxpr/ppermute | solution.py:16
  343.6 12.9 %collective-permute-start = (f32[32,2,512]{2,1,0:T(2,128)S(1)}, f32[32,2,512]{2,1,0:T(2,128)S(1)}, u32[]{:S(2)}, u32[]{:S(2)}) collective-permute-start(f32[32,2,512]{2,1,0:T(2,128)S(1)} %get-tuple-element.192), channel_id=1, source_target_pairs={{0,32},{32,64},{64,96},{96,128},{128,160},{160,192},{192,224},{224... | collective-permute-start | bytes 393224 | tf_op jit(solution)/shard_map/while/body/eval_jaxpr/ppermute | solution.py:16
  357.5 0.7 copy-start.7
